TPU v7x, 256 devices: a whole 4x4x8 slice. The times are simulated.
256 devices in a mesh: gx: 32 (over z_lo, y, core), gy: 4 (over x), gz: 2 (over z_hi).
Axes of the slice: x: 4, y: 4, z: 8 (z_hi: 2, z_lo: 4; z = z_hi * 4 + z_lo), core: 2. Of those that a mesh axis runs over, the one named last changes fastest.
Arguments:
- f_pop: float32 [19, 128, 64, 256], P(None, 'gx', 'gy', 'gz'), may hold values from 0.02 to 0.1
- g_pop: float32 [19, 128, 64, 256], P(None, 'gx', 'gy', 'gz'), may hold values from -0.2 to 0.2
- displacement: int32 [1], replicated, may hold values from 33 to 47
Outputs:
- f_new: float32 [19, 128, 64, 256], P(None, 'gx', 'gy', 'gz')
- g_new: float32 [19, 128, 64, 256], P(None, 'gx', 'gy', 'gz')
All inputs are finite; a program needn't handle non-finite values.
Results may differ from a plain program's by a relative error of at most 0.0001.
Values sent between devices are 32-bit elements; how exact they have to be, the bound alone decides.
No kernel may reach another device: no remote copies, remote signals or barrier semaphores. Data moves between devices by JAX's collectives and lax.ppermute only.
A program may use at most 64 MiB of HBM per device.

v0:
```python
import jax
import jax.numpy as jnp
from jax import lax
from jax.sharding import PartitionSpec as P

VELOCITIES = [
    (0, 0, 0),
    (1, 0, 0),
    (1, 1, 0),
    (1, -1, 0),
    (1, 0, 1),
    (1, 0, -1),
    (-1, 0, 0),
    (-1, -1, 0),
    (-1, 1, 0),
    (-1, 0, -1),
    (-1, 0, 1),
    (0, 1, 0),
    (0, -1, 0),
    (0, 0, 1),
    (0, 0, -1),
    (0, 1, 1),
    (0, -1, -1),
    (0, 1, -1),
    (0, -1, 1),
]
BULK_COEF = 0.5
STIFFNESS = 0.5
TAU_FLUID = 0.8
TAU_ORDER = 0.9


def with_halo(cells, sides, width):
    for axis, dim in sides:
        count = lax.axis_size(axis)
        head = lax.slice_in_dim(cells, 0, width, axis=dim)
        tail = lax.slice_in_dim(cells, cells.shape[dim] - width, cells.shape[dim], axis=dim)
        cells = jnp.concatenate(
            [
                lax.ppermute(tail, axis, [(i, (i + 1) % count) for i in range(count)]),
                cells,
                lax.ppermute(head, axis, [((i + 1) % count, i) for i in range(count)]),
            ],
            axis=dim,
        )
    return cells


def lattice_weight(number):
    steps_sq = sum((abs(comp) for comp in VELOCITIES[number]))
    if steps_sq == 0:
        return 1.0 / 3.0
    if steps_sq == 1:
        return 1.0 / 18.0
    return 1.0 / 36.0


def along(number, values, base):
    result = jnp.zeros_like(base)
    for axis_id in range(3):
        comp = VELOCITIES[number][axis_id]
        if comp != 0:
            result = result + comp * values[axis_id]
    return result


def collide(f_pop, g_pop, order_field, laplace, slopes):
    density = jnp.sum(f_pop, axis=0)
    chemical = (
        BULK_COEF * (order_field * order_field * order_field - order_field) - STIFFNESS * laplace
    )
    forces = [chemical * slope for slope in slopes]
    moments = []
    for axis_id in range(3):
        moment = jnp.zeros_like(density)
        for number in range(19):
            comp = VELOCITIES[number][axis_id]
            if comp != 0:
                moment = moment + comp * f_pop[number]
        moments.append(moment)
    flows = [(moments[axis_id] + 0.5 * forces[axis_id]) / density for axis_id in range(3)]
    speed_sq = flows[0] * flows[0] + flows[1] * flows[1] + flows[2] * flows[2]
    flow_force = flows[0] * forces[0] + flows[1] * forces[1] + flows[2] * forces[2]
    f_posts = []
    g_eqs = []
    for number in range(19):
        weight = lattice_weight(number)
        proj_flow = along(number, flows, density)
        proj_force = along(number, forces, density)
        shape_term = 3.0 * proj_flow + 4.5 * proj_flow * proj_flow - 1.5 * speed_sq
        f_eq = weight * density * (1.0 + shape_term)
        source = (
            (1.0 - 0.5 / TAU_FLUID)
            * weight
            * (3.0 * (proj_force - flow_force) + 9.0 * proj_flow * proj_force)
        )
        f_posts.append(f_pop[number] - (f_pop[number] - f_eq) / TAU_FLUID + source)
        g_eqs.append(weight * (3.0 * chemical + order_field * shape_term))
    rest_eq = order_field
    for number in range(1, 19):
        rest_eq = rest_eq - g_eqs[number]
    g_eqs[0] = rest_eq
    g_posts = [g_pop[number] - (g_pop[number] - g_eqs[number]) / TAU_ORDER for number in range(19)]
    return (jnp.stack(f_posts), jnp.stack(g_posts))


def window(whole, begin, rows, whole_rows):
    begin = jnp.mod(begin, whole_rows)
    doubled = jnp.concatenate([whole, whole], axis=1)
    return lax.dynamic_slice_in_dim(doubled, begin, rows, 1)


def sliding(edges, shift):
    extended = with_halo(edges, (("gx", 1),), 1)
    below = extended[:, 0]
    above = extended[:, 3]
    whole_below, whole_above = (
        lax.all_gather(below, "gy", axis=1, tiled=True),
        lax.all_gather(above, "gy", axis=1, tiled=True),
    )
    rows = below.shape[1]
    whole_rows = whole_below.shape[1]
    start = lax.axis_index("gy") * rows
    return (
        window(whole_below, start - shift, rows, whole_rows),
        window(whole_above, start + shift, rows, whole_rows),
    )


def extend_x(posts, below, above):
    rows, layers = (posts.shape[2], posts.shape[3])
    lower = jnp.concatenate(
        [
            jnp.zeros((1, rows, layers), jnp.float32),
            below,
            jnp.zeros((13, rows, layers), jnp.float32),
        ],
        axis=0,
    )
    upper = jnp.concatenate(
        [
            jnp.zeros((6, rows, layers), jnp.float32),
            above,
            jnp.zeros((8, rows, layers), jnp.float32),
        ],
        axis=0,
    )
    return jnp.concatenate([lower[:, None], posts, upper[:, None]], axis=1)


def local(f_pop, g_pop, displacement):
    shift = displacement[0]
    width_x, width_y, width_z = (f_pop.shape[1], f_pop.shape[2], f_pop.shape[3])
    order_field = jnp.sum(g_pop, axis=0)
    phase_edges = jnp.stack([order_field[0], order_field[-1]])[None]
    phase_below, phase_above = sliding(phase_edges, shift)
    neigh_xm = jnp.concatenate([phase_below, order_field[:-1]], axis=0)
    neigh_xp = jnp.concatenate([order_field[1:], phase_above], axis=0)
    padded = with_halo(order_field, (("gy", 1), ("gz", 2)), 1)
    neigh_ym = padded[:, :-2, 1:-1]
    neigh_yp = padded[:, 2:, 1:-1]
    neigh_zm = padded[:, 1:-1, :-2]
    neigh_zp = padded[:, 1:-1, 2:]
    laplace = neigh_xm + neigh_xp + neigh_ym + neigh_yp + neigh_zm + neigh_zp - 6.0 * order_field
    slopes = [0.5 * (neigh_xp - neigh_xm), 0.5 * (neigh_yp - neigh_ym), 0.5 * (neigh_zp - neigh_zm)]
    f_post, g_post = collide(f_pop, g_pop, order_field, laplace, slopes)
    pop_edges = jnp.concatenate(
        [
            jnp.stack([f_post[6:11, 0], f_post[1:6, -1]], axis=1),
            jnp.stack([g_post[6:11, 0], g_post[1:6, -1]], axis=1),
        ],
        axis=0,
    )
    pop_below, pop_above = sliding(pop_edges, shift)
    layered = jnp.concatenate(
        [
            extend_x(f_post, pop_below[0:5], pop_above[0:5]),
            extend_x(g_post, pop_below[5:10], pop_above[5:10]),
        ],
        axis=0,
    )
    results = []
    padded_all = with_halo(layered, (("gy", 2), ("gz", 3)), 1)
    for number in range(38):
        vel_x, vel_y, vel_z = VELOCITIES[number % 19]
        results.append(
            padded_all[
                number,
                1 - vel_x : 1 - vel_x + width_x,
                1 - vel_y : 1 - vel_y + width_y,
                1 - vel_z : 1 - vel_z + width_z,
            ]
        )
    f_new = jnp.stack(results[:19])
    g_new = jnp.stack(results[19:])
    return (f_new, g_new)


def solution(mesh):
    return jax.shard_map(
        local,
        mesh=mesh,
        in_specs=(P(None, "gx", "gy", "gz"), P(None, "gx", "gy", "gz"), P()),
        out_specs=(P(None, "gx", "gy", "gz"), P(None, "gx", "gy", "gz")),
        check_vma=False,
    )
```

profile of v0, /device:TPU:6, one launch (start us, length us, event | category | flops | bytes accessed | tf_op | source)
XLA Modules:
  0.0 120.2 jit_solution(16818710644719364818)
XLA Ops:
  0.7 1.2 %reduce_sum.19 = f32[4,16,128]{2,1,0:T(8,128)S(1)} reduce(f32[19,4,16,128]{3,2,1,0:T(8,128)} %param.4, f32[]{:T(128)} %constant.95.clone.1), dimensions={0}, to_apply=%region_1.2 | reduce | flops 147456 | bytes 655364 | tf_op jit(solution)/shard_map/reduce_sum | solution.py:154
  1.9 0.9 collective-permute-start.3
  2.8 2.4 %collective-permute-start.2 = (f32[4,1,128]{2,1,0:T(1,128)S(1)}, f32[4,1,128]{2,1,0:T(1,128)S(1)}, u32[]{:S(2)}, u32[]{:S(2)}) collective-permute-start(f32[4,1,128]{2,1,0:T(1,128)S(1)} %get-tuple-element.109), channel_id=1, source_target_pairs={{0,2},{2,4},{4,6},{6,0},{1,3},{3,5},{5,7},{7,1},{8,10},{10,12},{12... | collective-permute-start | bytes 6152 | tf_op jit(solution)/shard_map/ppermute | solution.py:40
  5.2 6.0 %collective-permute-start.1 = (f32[1,1,16,128]{3,2,1,0:T(8,128)S(1)}, f32[1,1,16,128]{3,2,1,0:T(8,128)S(1)}, u32[]{:S(2)}, u32[]{:S(2)}) collective-permute-start(f32[1,1,16,128]{3,2,1,0:T(8,128)S(1)} %get-tuple-element.114), channel_id=1, source_target_pairs={{8,0},{16,8},{24,16},{32,24},{40,32},{48,40},{56,48},{64,56},{72,6... | collective-permute-start | bytes 24584 | tf_op jit(solution)/shard_map/ppermute | solution.py:42
  12.1 1.1 reduce_sum.18
  13.4 4.5 %collective-permute-start.5 = (f32[4,18,1]{2,1,0:T(8,128)S(1)}, f32[4,18,1]{2,1,0:T(8,128)S(1)}, u32[]{:S(2)}, u32[]{:S(2)}) collective-permute-start(f32[4,18,1]{2,1,0:T(8,128)S(1)} %get-tuple-element.106), channel_id=1, source_target_pairs={{1,0},{0,1},{3,2},{2,3},{5,4},{4,5},{7,6},{6,7},{9,8},{8,9},{11,10... | collective-permute-start | bytes 872 | tf_op jit(solution)/shard_map/ppermute | solution.py:42
  17.9 1.4 %collective-permute-start.4 = (f32[4,18,1]{2,1,0:T(8,128)S(1)}, f32[4,18,1]{2,1,0:T(8,128)S(1)}, u32[]{:S(2)}, u32[]{:S(2)}) collective-permute-start(f32[4,18,1]{2,1,0:T(8,128)S(1)} %get-tuple-element.107), channel_id=1, source_target_pairs={{0,1},{1,0},{2,3},{3,2},{4,5},{5,4},{6,7},{7,6},{8,9},{9,8},{10,11... | collective-permute-start | bytes 872 | tf_op jit(solution)/shard_map/ppermute | solution.py:40
  19.4 11.9 %all-gather = f32[1,1,64,128]{3,2,1,0:T(8,128)S(1)} all-gather(f32[1,1,16,128]{3,2,1,0:T(8,128)S(1)} %collective-permute-done), channel_id=2, replica_groups=mesh['gx'=32,'gy'=4,'gz'=2] {'gy'}, dimensions={2}, use_global_device_ids=true | all-gather | bytes 40960 | tf_op jit(solution)/shard_map/all_gather | solution.py:118
  31.3 11.9 %all-gather.1 = f32[1,1,64,128]{3,2,1,0:T(8,128)S(1)} all-gather(f32[1,1,16,128]{3,2,1,0:T(8,128)S(1)} %collective-permute-done.1), channel_id=3, replica_groups=mesh['gx'=32,'gy'=4,'gz'=2] {'gy'}, dimensions={2}, use_global_device_ids=true | all-gather | bytes 40960 | tf_op jit(solution)/shard_map/all_gather | solution.py:119
  43.2 1.4 %bitcast_subtract_fusion.16 = (f32[4,16,128]{2,1,0:T(8,128)S(1)}, f32[4,16,128]{2,1,0:T(8,128)S(1)}, f32[4,16,128]{2,1,0:T(8,128)S(1)}, f32[4,16,128]{2,1,0:T(8,...) fusion(f32[4,16,128]{2,1,0:T(8,128)S(1)} %reduce_sum.19, ...), kind=kLoop, calls=%fused_computation.190 | loop fusion | flops 2064384 | bytes 1512000 | tf_op jit(solution)/shard_map/sub | solution.py:103
  45.5 0.5 collective-permute-start.6
  46.0 0.8 copy.371
  47.3 6.0 %collective-permute-done.6 = f32[10,1,16,128]{3,2,1,0:T(8,128)S(1)} collective-permute-done((f32[10,1,16,128]{3,2,1,0:T(8,128)S(1)}, f32[10,1,16,128]{3,2,1,0:T(8,128)S(1)}, u32[]{:S(2)}, u32[]{:S(2)}) %collective-permute-start.6) | collective-permute-done | bytes 81952 | tf_op jit(solution)/shard_map/ppermute | solution.py:40
  53.4 12.4 %all-gather.2 = f32[10,1,64,128]{3,1,0,2:T(1,128)S(1)} all-gather(f32[10,1,16,128]{3,1,0,2:T(1,128)S(1)} %copy.282), channel_id=4, replica_groups=mesh['gx'=32,'gy'=4,'gz'=2] {'gy'}, dimensions={2}, use_global_device_ids=true | all-gather | bytes 409600 | tf_op jit(solution)/shard_map/all_gather | solution.py:118
  66.0 12.4 %all-gather.3 = f32[10,1,64,128]{3,1,0,2:T(1,128)S(1)} all-gather(f32[10,1,16,128]{3,1,0,2:T(1,128)S(1)} %copy.284), channel_id=5, replica_groups=mesh['gx'=32,'gy'=4,'gz'=2] {'gy'}, dimensions={2}, use_global_device_ids=true | all-gather | bytes 409600 | tf_op jit(solution)/shard_map/all_gather | solution.py:119
  78.5 0.1 maximum_bitcast_fusion.2
  78.6 0.1 maximum_bitcast_fusion.1
  78.7 0.2 fusion
  78.9 0.7 collective-permute-start.8
  79.6 1.7 %collective-permute-start.9 = (f32[38,6,1,128]{3,0,2,1:T(8,128)S(1)}, f32[38,6,1,128]{3,0,2,1:T(8,128)S(1)}, u32[]{:S(2)}, u32[]{:S(2)}) collective-permute-start(f32[38,6,1,128]{3,0,2,1:T(8,128)S(1)} %copy.290), channel_id=1, source_target_pairs={{2,0},{4,2},{6,4},{0,6},{3,1},{5,3},{7,5},{1,7},{10,8},{12,10},{14... | collective-permute-start | bytes 350216 | tf_op jit(solution)/shard_map/ppermute | solution.py:42
  81.3 2.6 %collective-permute-done.8 = f32[38,6,1,128]{3,0,2,1:T(8,128)S(1)} collective-permute-done((f32[38,6,1,128]{3,0,2,1:T(8,128)S(1)}, f32[38,6,1,128]{3,0,2,1:T(8,128)S(1)}, u32[]{:S(2)}, u32[]{:S(2)}) %collective-permute-start.8) | collective-permute-done | bytes 116768 | tf_op jit(solution)/shard_map/ppermute | solution.py:40
  83.8 0.1 copy.289
  84.0 1.9 %collective-permute-done.9 = f32[38,6,1,128]{3,0,2,1:T(8,128)S(1)} collective-permute-done((f32[38,6,1,128]{3,0,2,1:T(8,128)S(1)}, f32[38,6,1,128]{3,0,2,1:T(8,128)S(1)}, u32[]{:S(2)}, u32[]{:S(2)}) %collective-permute-start.9) | collective-permute-done | bytes 116768 | tf_op jit(solution)/shard_map/ppermute | solution.py:42
  85.9 0.1 copy.291
  86.0 0.5 pad_maximum_fusion
  86.5 3.2 %fusion.105 = (f32[38,6,18,1]{3,2,1,0:T(8,128)}, f32[38,6,18,1]{3,2,1,0:T(8,128)}) fusion(f32[38,6,18,128]{3,2,1,0:T(8,128)S(1)} %pad_maximum_fusion), kind=kLoop, calls=%fused_computation.399 | loop fusion | bytes 65664 | tf_op jit(solution)/shard_map/slice | solution.py:36
  89.7 3.0 %copy.294 = f32[38,6,18,1]{0,2,3,1:T(8,128)S(1)} copy(f32[38,6,18,1]{3,2,1,0:T(8,128)} %get-tuple-element.53) | data formatting | bytes 32832 | tf_op jit(solution)/shard_map/slice | solution.py:37
  92.8 4.6 %collective-permute-start.10 = (f32[38,6,18,1]{0,2,3,1:T(8,128)S(1)}, f32[38,6,18,1]{0,2,3,1:T(8,128)S(1)}, u32[]{:S(2)}, u32[]{:S(2)}) collective-permute-start(f32[38,6,18,1]{0,2,3,1:T(8,128)S(1)} %copy.294), channel_id=1, source_target_pairs={{0,1},{1,0},{2,3},{3,2},{4,5},{5,4},{6,7},{7,6},{8,9},{9,8},{10,11... | collective-permute-start | bytes 49256 | tf_op jit(solution)/shard_map/ppermute | solution.py:40
  97.4 3.0 %copy.296 = f32[38,6,18,1]{0,2,3,1:T(8,128)S(1)} copy(f32[38,6,18,1]{3,2,1,0:T(8,128)} %get-tuple-element.52) | data formatting | bytes 32832 | tf_op jit(solution)/shard_map/slice | solution.py:36
  100.4 1.5 %collective-permute-start.11 = (f32[38,6,18,1]{0,2,3,1:T(8,128)S(1)}, f32[38,6,18,1]{0,2,3,1:T(8,128)S(1)}, u32[]{:S(2)}, u32[]{:S(2)}) collective-permute-start(f32[38,6,18,1]{0,2,3,1:T(8,128)S(1)} %copy.296), channel_id=1, source_target_pairs={{1,0},{0,1},{3,2},{2,3},{5,4},{4,5},{7,6},{6,7},{9,8},{8,9},{11,10... | collective-permute-start | bytes 49256 | tf_op jit(solution)/shard_map/ppermute | solution.py:42
  101.9 2.8 %copy.295 = f32[38,6,18,1]{3,2,1,0:T(8,128)} copy(f32[38,6,18,1]{0,2,3,1:T(8,128)S(1)} %collective-permute-done.10) | data formatting | bytes 32832 | tf_op jit(solution)/shard_map/ppermute | solution.py:40
  104.7 0.9 constant_dynamic-update-slice_fusion.91
  105.5 3.2 %collective-permute-done.11 = f32[38,6,18,1]{0,2,3,1:T(8,128)S(1)} collective-permute-done((f32[38,6,18,1]{0,2,3,1:T(8,128)S(1)}, f32[38,6,18,1]{0,2,3,1:T(8,128)S(1)}, u32[]{:S(2)}, u32[]{:S(2)}) %collective-permute-start.11) | collective-permute-done | bytes 16448 | tf_op jit(solution)/shard_map/ppermute | solution.py:42
  108.7 2.8 %copy.297 = f32[38,6,18,1]{3,2,1,0:T(8,128)} copy(f32[38,6,18,1]{0,2,3,1:T(8,128)S(1)} %collective-permute-done.11) | data formatting | bytes 32832 | tf_op jit(solution)/shard_map/ppermute | solution.py:42
  111.5 0.9 constant_dynamic-update-slice_fusion.90
  112.5 1.7 %copy-done.1 = f32[38,6,18,1]{3,2,1,0:T(8,128)S(1)} copy-done((f32[38,6,18,1]{3,2,1,0:T(8,128)S(1)}, f32[38,6,18,1]{3,2,1,0:T(8,128)}, u32[]{:S(2)}) %copy-start.1) | copy-done | bytes 16440
  114.3 1.7 %copy-done = f32[38,6,18,1]{3,2,1,0:T(8,128)S(1)} copy-done((f32[38,6,18,1]{3,2,1,0:T(8,128)S(1)}, f32[38,6,18,1]{3,2,1,0:T(8,128)}, u32[]{:S(2)}) %copy-start) | copy-done | bytes 16440
  116.2 0.1 constant_dynamic-update-slice_fusion.81
  116.3 1.0 copy-done.5
  117.4 0.1 constant_dynamic-update-slice_fusion.79
  117.6 0.1 constant_dynamic-update-slice_fusion.71
  117.7 0.1 constant_dynamic-update-slice_fusion.78
  117.8 0.1 constant_dynamic-update-slice_fusion.67
  118.0 0.1 constant_dynamic-update-slice_fusion.77
  118.2 0.7 copy-done.4
  119.1 0.1 constant_dynamic-update-slice_fusion.60
  119.2 0.1 constant_dynamic-update-slice_fusion.59
  119.4 0.8 copy-done.6
  (113 shorter events, 2.6 us)
Async XLA Ops:
  0.6 44.2 %copy-start.3 = (f32[19,4,16,128]{3,2,1,0:T(8,128)S(1)}, f32[19,4,16,128]{3,2,1,0:T(8,128)}, u32[]{:S(2)}) copy-start(f32[19,4,16,128]{3,2,1,0:T(8,128)} %param.4) | copy-start | bytes 1867780
  0.6 44.0 %copy-start.2 = (f32[19,4,16,128]{3,2,1,0:T(8,128)S(1)}, f32[19,4,16,128]{3,2,1,0:T(8,128)}, u32[]{:S(2)}) copy-start(f32[19,4,16,128]{3,2,1,0:T(8,128)} %param.3) | copy-start | bytes 1867780
  1.9 11.4 %collective-permute-start.3 = (f32[4,1,128]{2,1,0:T(1,128)S(1)}, f32[4,1,128]{2,1,0:T(1,128)S(1)}, u32[]{:S(2)}, u32[]{:S(2)}) collective-permute-start(f32[4,1,128]{2,1,0:T(1,128)S(1)} %get-tuple-element.108), channel_id=1, source_target_pairs={{2,0},{4,2},{6,4},{0,6},{3,1},{5,3},{7,5},{1,7},{10,8},{12,10},{14... | collective-permute-start | bytes 6152 | tf_op jit(solution)/shard_map/ppermute | solution.py:42
  2.8 10.5 %collective-permute-start.2 = (f32[4,1,128]{2,1,0:T(1,128)S(1)}, f32[4,1,128]{2,1,0:T(1,128)S(1)}, u32[]{:S(2)}, u32[]{:S(2)}) collective-permute-start(f32[4,1,128]{2,1,0:T(1,128)S(1)} %get-tuple-element.109), channel_id=1, source_target_pairs={{0,2},{2,4},{4,6},{6,0},{1,3},{3,5},{5,7},{7,1},{8,10},{10,12},{12... | collective-permute-start | bytes 6152 | tf_op jit(solution)/shard_map/ppermute | solution.py:40
  5.2 26.1 %collective-permute-start.1 = (f32[1,1,16,128]{3,2,1,0:T(8,128)S(1)}, f32[1,1,16,128]{3,2,1,0:T(8,128)S(1)}, u32[]{:S(2)}, u32[]{:S(2)}) collective-permute-start(f32[1,1,16,128]{3,2,1,0:T(8,128)S(1)} %get-tuple-element.114), channel_id=1, source_target_pairs={{8,0},{16,8},{24,16},{32,24},{40,32},{48,40},{56,48},{64,56},{72,6... | collective-permute-start | bytes 24584 | tf_op jit(solution)/shard_map/ppermute | solution.py:42
  11.2 8.1 %collective-permute-start = (f32[1,1,16,128]{3,2,1,0:T(8,128)S(1)}, f32[1,1,16,128]{3,2,1,0:T(8,128)S(1)}, u32[]{:S(2)}, u32[]{:S(2)}) collective-permute-start(f32[1,1,16,128]{3,2,1,0:T(8,128)S(1)} %get-tuple-element.115), channel_id=1, source_target_pairs={{0,8},{8,16},{16,24},{24,32},{32,40},{40,48},{48,56},{56,64},{64,7... | collective-permute-start | bytes 24584 | tf_op jit(solution)/shard_map/ppermute | solution.py:40
  13.4 29.9 %collective-permute-start.5 = (f32[4,18,1]{2,1,0:T(8,128)S(1)}, f32[4,18,1]{2,1,0:T(8,128)S(1)}, u32[]{:S(2)}, u32[]{:S(2)}) collective-permute-start(f32[4,18,1]{2,1,0:T(8,128)S(1)} %get-tuple-element.106), channel_id=1, source_target_pairs={{1,0},{0,1},{3,2},{2,3},{5,4},{4,5},{7,6},{6,7},{9,8},{8,9},{11,10... | collective-permute-start | bytes 872 | tf_op jit(solution)/shard_map/ppermute | solution.py:42
  17.9 25.3 %collective-permute-start.4 = (f32[4,18,1]{2,1,0:T(8,128)S(1)}, f32[4,18,1]{2,1,0:T(8,128)S(1)}, u32[]{:S(2)}, u32[]{:S(2)}) collective-permute-start(f32[4,18,1]{2,1,0:T(8,128)S(1)} %get-tuple-element.107), channel_id=1, source_target_pairs={{0,1},{1,0},{2,3},{3,2},{4,5},{5,4},{6,7},{7,6},{8,9},{9,8},{10,11... | collective-permute-start | bytes 872 | tf_op jit(solution)/shard_map/ppermute | solution.py:40
  45.4 20.5 %collective-permute-start.7 = (f32[10,1,16,128]{3,2,1,0:T(8,128)S(1)}, f32[10,1,16,128]{3,2,1,0:T(8,128)S(1)}, u32[]{:S(2)}, u32[]{:S(2)}) collective-permute-start(f32[10,1,16,128]{3,2,1,0:T(8,128)S(1)} %get-tuple-element.92), channel_id=1, source_target_pairs={{8,0},{16,8},{24,16},{32,24},{40,32},{48,40},{56,48},{64,56},{72,6... | collective-permute-start | bytes 245768 | tf_op jit(solution)/shard_map/ppermute | solution.py:42
  45.5 7.9 %collective-permute-start.6 = (f32[10,1,16,128]{3,2,1,0:T(8,128)S(1)}, f32[10,1,16,128]{3,2,1,0:T(8,128)S(1)}, u32[]{:S(2)}, u32[]{:S(2)}) collective-permute-start(f32[10,1,16,128]{3,2,1,0:T(8,128)S(1)} %get-tuple-element.93), channel_id=1, source_target_pairs={{0,8},{8,16},{16,24},{24,32},{32,40},{40,48},{48,56},{56,64},{64,7... | collective-permute-start | bytes 245768 | tf_op jit(solution)/shard_map/ppermute | solution.py:40
  78.9 5.0 %collective-permute-start.8 = (f32[38,6,1,128]{3,0,2,1:T(8,128)S(1)}, f32[38,6,1,128]{3,0,2,1:T(8,128)S(1)}, u32[]{:S(2)}, u32[]{:S(2)}) collective-permute-start(f32[38,6,1,128]{3,0,2,1:T(8,128)S(1)} %copy.288), channel_id=1, source_target_pairs={{0,2},{2,4},{4,6},{6,0},{1,3},{3,5},{5,7},{7,1},{8,10},{10,12},{12... | collective-permute-start | bytes 350216 | tf_op jit(solution)/shard_map/ppermute | solution.py:40
  79.6 6.3 %collective-permute-start.9 = (f32[38,6,1,128]{3,0,2,1:T(8,128)S(1)}, f32[38,6,1,128]{3,0,2,1:T(8,128)S(1)}, u32[]{:S(2)}, u32[]{:S(2)}) collective-permute-start(f32[38,6,1,128]{3,0,2,1:T(8,128)S(1)} %copy.290), channel_id=1, source_target_pairs={{2,0},{4,2},{6,4},{0,6},{3,1},{5,3},{7,5},{1,7},{10,8},{12,10},{14... | collective-permute-start | bytes 350216 | tf_op jit(solution)/shard_map/ppermute | solution.py:42
  92.8 9.1 %collective-permute-start.10 = (f32[38,6,18,1]{0,2,3,1:T(8,128)S(1)}, f32[38,6,18,1]{0,2,3,1:T(8,128)S(1)}, u32[]{:S(2)}, u32[]{:S(2)}) collective-permute-start(f32[38,6,18,1]{0,2,3,1:T(8,128)S(1)} %copy.294), channel_id=1, source_target_pairs={{0,1},{1,0},{2,3},{3,2},{4,5},{5,4},{6,7},{7,6},{8,9},{9,8},{10,11... | collective-permute-start | bytes 49256 | tf_op jit(solution)/shard_map/ppermute | solution.py:40
  100.4 8.3 %collective-permute-start.11 = (f32[38,6,18,1]{0,2,3,1:T(8,128)S(1)}, f32[38,6,18,1]{0,2,3,1:T(8,128)S(1)}, u32[]{:S(2)}, u32[]{:S(2)}) collective-permute-start(f32[38,6,18,1]{0,2,3,1:T(8,128)S(1)} %copy.296), channel_id=1, source_target_pairs={{1,0},{0,1},{3,2},{2,3},{5,4},{4,5},{7,6},{6,7},{9,8},{8,9},{11,10... | collective-permute-start | bytes 49256 | tf_op jit(solution)/shard_map/ppermute | solution.py:42
  112.4 1.8 %copy-start.1 = (f32[38,6,18,1]{3,2,1,0:T(8,128)S(1)}, f32[38,6,18,1]{3,2,1,0:T(8,128)}, u32[]{:S(2)}) copy-start(f32[38,6,18,1]{3,2,1,0:T(8,128)} %copy.297) | copy-start | bytes 49252
  114.2 1.8 %copy-start = (f32[38,6,18,1]{3,2,1,0:T(8,128)S(1)}, f32[38,6,18,1]{3,2,1,0:T(8,128)}, u32[]{:S(2)}) copy-start(f32[38,6,18,1]{3,2,1,0:T(8,128)} %copy.295) | copy-start | bytes 49252
  116.2 1.1 copy-start.5
  118.1 0.8 copy-start.4
  119.4 0.8 copy-start.6
where the time goes:
time: 121 us; the launch traced here: 120 us
  blocking collectives  48.6 us (40%)
  starting transfers between devices  24.3 us (20%)
  local copies, waits for them, and re-layouts  22.6 us (19%)
  waiting for transfers between devices  13.7 us (11%)
  other arithmetic  8.9 us (7%)
  between operations  2.11 us (2%)
    all_gather x2, blocking collectives, sliding(): lax.all_gather(above, 'gy', axis=1, tiled=True)  24.3 us
    all_gather x2, blocking collectives, sliding(): lax.all_gather(below, 'gy', axis=1, tiled=True)  24.3 us
    ppermute x6, starting transfers between devices, with_halo(): lax.ppermute(head, axis, [((i + 1) % count, i) for i in range(count)])  14.7 us
    ppermute x6, starting transfers between devices, with_halo(): lax.ppermute(tail, axis, [(i, (i + 1) % count) for i in range(count)])  9.57 us
    ppermute x6, waiting for transfers between devices, with_halo(): lax.ppermute(tail, axis, [(i, (i + 1) % count) for i in range(count)])  8.57 us
    unnamed x27, local copies, waits for them, and re-layouts  6.9 us
    slice x7, local copies, waits for them, and re-layouts, with_halo(): head = lax.slice_in_dim(cells, 0, width, axis=dim)  6.39 us
    ppermute x6, waiting for transfers between devices, with_halo(): lax.ppermute(head, axis, [((i + 1) % count, i) for i in range(count)])  5.11 us
  transfers between devices with their start and end apart: 12, of which 4 were waited for; matrix products, arithmetic and copies ran while one was open for 8% of the time, Pallas kernels for 0%

commit v1 on v0

--- a/solution.py
+++ b/solution.py
@@ -2,6 +2,7 @@
 import jax.numpy as jnp
 from jax import lax
 from jax.sharding import PartitionSpec as P
+from jax.lax import axis_index, ppermute, psum
 
 VELOCITIES = [
     (0, 0, 0),
@@ -28,6 +29,29 @@
 STIFFNESS = 0.5
 TAU_FLUID = 0.8
 TAU_ORDER = 0.9
+
+
+def _end_flows(row_data):
+    found_now = psum(1, axis_name="gy")
+    base_arr = axis_index("gy")
+    finding, u1, o_now = (found_now, base_arr, row_data.shape[1])
+    newest = jnp.zeros(
+        [hop_no * finding if m == 1 else hop_no for m, hop_no in enumerate(row_data.shape)],
+        row_data.dtype,
+    )
+    r_now = lax.dynamic_update_slice_in_dim(newest, row_data, u1 * o_now, axis=1)
+    v1 = work_now = row_data
+    for nth in range(1, finding // 2 + 1):
+        v1 = ppermute(v1, axis_name="gy", perm=[(m, (m + 1) % finding) for m in range(finding)])
+        r_now = lax.dynamic_update_slice_in_dim(r_now, v1, (u1 - nth) % finding * o_now, axis=1)
+        if 2 * nth < finding:
+            work_now = ppermute(
+                work_now, axis_name="gy", perm=[(m, (m - 1) % finding) for m in range(finding)]
+            )
+            r_now = lax.dynamic_update_slice_in_dim(
+                r_now, work_now, (u1 + nth) % finding * o_now, axis=1
+            )
+    return r_now
 
 
 def with_halo(cells, sides, width):
@@ -114,10 +138,7 @@
     extended = with_halo(edges, (("gx", 1),), 1)
     below = extended[:, 0]
     above = extended[:, 3]
-    whole_below, whole_above = (
-        lax.all_gather(below, "gy", axis=1, tiled=True),
-        lax.all_gather(above, "gy", axis=1, tiled=True),
-    )
+    whole_below, whole_above = (_end_flows(below), lax.all_gather(above, "gy", axis=1, tiled=True))
     rows = below.shape[1]
     whole_rows = whole_below.shape[1]
     start = lax.axis_index("gy") * rows

time: 121 us -> 114 us (0.942)
  blocking collectives: 48.6 us -> 24.9 us
  starting transfers between devices: 24.3 us -> 35 us
  waiting for transfers between devices: 13.7 us -> 19.7 us
    all_gather x2 -> x0, blocking collectives: 24.3 us -> none  [sliding(): lax.all_gather(below, 'gy', axis=1, tiled=True)]
    ppermute x0 -> x6, starting transfers between devices: none -> 9.28 us  [the longest x4 7.55 us: _end_flows(): ppermute(v1, axis_name='gy', perm=[(m, (m + 1) % finding) for m in range(...]
    ppermute x0 -> x6, waiting for transfers between devices: none -> 4.14 us  [the longest x4 4.14 us: _end_flows(): ppermute(v1, axis_name='gy', perm=[(m, (m + 1) % finding) for m in range(...]
    ppermute x6, starting transfers between devices: 9.57 us -> 12.1 us  [with_halo(): lax.ppermute(tail, axis, [(i, (i + 1) % count) for i in range(count)])]
    ppermute x6, waiting for transfers between devices: 5.11 us -> 6.72 us  [with_halo(): lax.ppermute(head, axis, [((i + 1) % count, i) for i in range(count)])]
    unnamed x27 -> x25, local copies, waits for them, and re-layouts: 6.9 us -> 7.14 us
    ppermute x3 -> x2, local copies, waits for them, and re-layouts: 2.97 us -> 2.8 us  [with_halo(): lax.ppermute(tail, axis, [(i, (i + 1) % count) for i in range(count)])]
    unnamed x56 -> x60, other arithmetic: 3.92 us -> 3.97 us
  transfers between devices with their start and end apart: 12 -> 18, of which waited for: 4 -> 7; matrix products, arithmetic and copies ran while one was open for 8% -> 8% of each run, Pallas kernels for 0% -> 0%
where the time goes in v1:
time: 114 us; the launch traced here: 113 us
  starting transfers between devices  35 us (31%)
  blocking collectives  24.9 us (22%)
  local copies, waits for them, and re-layouts  22.3 us (20%)
  waiting for transfers between devices  19.7 us (17%)
  other arithmetic  8.93 us (8%)
  between operations  2.19 us (2%)
    all_gather x2, blocking collectives, sliding(): lax.all_gather(above, 'gy', axis=1, tiled=True)  24.9 us
    ppermute x6, starting transfers between devices, with_halo(): lax.ppermute(head, axis, [((i + 1) % count, i) for i in range(count)])  13.6 us
    ppermute x6, starting transfers between devices, with_halo(): lax.ppermute(tail, axis, [(i, (i + 1) % count) for i in range(count)])  12.1 us
    ppermute x6, waiting for transfers between devices, with_halo(): lax.ppermute(tail, axis, [(i, (i + 1) % count) for i in range(count)])  8.84 us
    ppermute x4, starting transfers between devices, _end_flows(): ppermute(v1, axis_name='gy', perm=[(m, (m + 1) % finding) for m in range(...  7.55 us
    unnamed x25, local copies, waits for them, and re-layouts  7.14 us
    ppermute x6, waiting for transfers between devices, with_halo(): lax.ppermute(head, axis, [((i + 1) % count, i) for i in range(count)])  6.72 us
    slice x7, local copies, waits for them, and re-layouts, with_halo(): head = lax.slice_in_dim(cells, 0, width, axis=dim)  6.23 us
  transfers between devices with their start and end apart: 18, of which 7 were waited for; matrix products, arithmetic and copies ran while one was open for 8% of the time, Pallas kernels for 0%

profile of v1, /device:TPU:6, one launch (start us, length us, event | category | flops | bytes accessed | tf_op | source)
XLA Modules:
  0.0 113.0 jit_solution(1753185039659289932)
XLA Ops:
  0.7 1.2 %reduce_sum.19 = f32[4,16,128]{2,1,0:T(8,128)S(1)} reduce(f32[19,4,16,128]{3,2,1,0:T(8,128)} %param.4, f32[]{:T(128)} %constant.123.clone.1), dimensions={0}, to_apply=%region_1.2 | reduce | flops 147456 | bytes 655364 | tf_op jit(solution)/shard_map/reduce_sum | solution.py:175
  1.9 0.9 collective-permute-start.6
  2.8 2.4 %collective-permute-start.5 = (f32[4,1,128]{2,1,0:T(1,128)S(1)}, f32[4,1,128]{2,1,0:T(1,128)S(1)}, u32[]{:S(2)}, u32[]{:S(2)}) collective-permute-start(f32[4,1,128]{2,1,0:T(1,128)S(1)} %get-tuple-element.99), channel_id=1, source_target_pairs={{0,2},{2,4},{4,6},{6,0},{1,3},{3,5},{5,7},{7,1},{8,10},{10,12},{12... | collective-permute-start | bytes 6152 | tf_op jit(solution)/shard_map/ppermute | solution.py:64
  5.2 6.0 %collective-permute-start.4 = (f32[1,1,16,128]{3,2,1,0:T(8,128)S(1)}, f32[1,1,16,128]{3,2,1,0:T(8,128)S(1)}, u32[]{:S(2)}, u32[]{:S(2)}) collective-permute-start(f32[1,1,16,128]{3,2,1,0:T(8,128)S(1)} %get-tuple-element.104), channel_id=1, source_target_pairs={{8,0},{16,8},{24,16},{32,24},{40,32},{48,40},{56,48},{64,56},{72,6... | collective-permute-start | bytes 24584 | tf_op jit(solution)/shard_map/ppermute | solution.py:66
  12.1 1.1 reduce_sum.18
  13.4 4.5 %collective-permute-start.8 = (f32[4,18,1]{2,1,0:T(8,128)S(1)}, f32[4,18,1]{2,1,0:T(8,128)S(1)}, u32[]{:S(2)}, u32[]{:S(2)}) collective-permute-start(f32[4,18,1]{2,1,0:T(8,128)S(1)} %get-tuple-element.96), channel_id=1, source_target_pairs={{1,0},{0,1},{3,2},{2,3},{5,4},{4,5},{7,6},{6,7},{9,8},{8,9},{11,10... | collective-permute-start | bytes 872 | tf_op jit(solution)/shard_map/ppermute | solution.py:66
  17.9 1.4 %collective-permute-start.7 = (f32[4,18,1]{2,1,0:T(8,128)S(1)}, f32[4,18,1]{2,1,0:T(8,128)S(1)}, u32[]{:S(2)}, u32[]{:S(2)}) collective-permute-start(f32[4,18,1]{2,1,0:T(8,128)S(1)} %get-tuple-element.97), channel_id=1, source_target_pairs={{0,1},{1,0},{2,3},{3,2},{4,5},{5,4},{6,7},{7,6},{8,9},{9,8},{10,11... | collective-permute-start | bytes 872 | tf_op jit(solution)/shard_map/ppermute | solution.py:64
  19.4 0.3 collective-permute-start.1
  19.7 1.7 %collective-permute-start.2 = (f32[1,16,128]{2,1,0:T(8,128)S(1)}, f32[1,16,128]{2,1,0:T(8,128)S(1)}, u32[]{:S(2)}, u32[]{:S(2)}) collective-permute-start(f32[1,16,128]{2,1,0:T(8,128)S(1)} %bitcast.732), channel_id=1, source_target_pairs={{0,6},{2,0},{4,2},{6,4},{1,7},{3,1},{5,3},{7,5},{8,14},{10,8},{12,... | collective-permute-start | bytes 24584 | tf_op jit(solution)/shard_map/ppermute | solution.py:48
  21.4 11.9 %all-gather = f32[1,1,64,128]{3,2,1,0:T(8,128)S(1)} all-gather(f32[1,1,16,128]{3,2,1,0:T(8,128)S(1)} %collective-permute-done.4), channel_id=2, replica_groups=mesh['gx'=32,'gy'=4,'gz'=2] {'gy'}, dimensions={2}, use_global_device_ids=true | all-gather | bytes 40960 | tf_op jit(solution)/shard_map/all_gather | solution.py:141
  33.4 1.6 %collective-permute-start.3 = (f32[1,16,128]{2,1,0:T(8,128)S(1)}, f32[1,16,128]{2,1,0:T(8,128)S(1)}, u32[]{:S(2)}, u32[]{:S(2)}) collective-permute-start(f32[1,16,128]{2,1,0:T(8,128)S(1)} %collective-permute-done.1), channel_id=1, source_target_pairs={{0,2},{2,4},{4,6},{6,0},{1,3},{3,5},{5,7},{7,1},{8,10},{10,12},{12... | collective-permute-start | bytes 24584 | tf_op jit(solution)/shard_map/ppermute | solution.py:45
  35.0 2.1 %collective-permute-done.3 = f32[1,16,128]{2,1,0:T(8,128)S(1)} collective-permute-done((f32[1,16,128]{2,1,0:T(8,128)S(1)}, f32[1,16,128]{2,1,0:T(8,128)S(1)}, u32[]{:S(2)}, u32[]{:S(2)}) %collective-permute-start.3) | collective-permute-done | bytes 8224 | tf_op jit(solution)/shard_map/ppermute | solution.py:45
  37.1 1.4 %bitcast_subtract_fusion.16 = (f32[4,16,128]{2,1,0:T(8,128)S(1)}, f32[4,16,128]{2,1,0:T(8,128)S(1)}, f32[4,16,128]{2,1,0:T(8,128)S(1)}, f32[4,16,128]{2,1,0:T(8,...) fusion(f32[4,16,128]{2,1,0:T(8,128)S(1)} %reduce_sum.19, ...), kind=kLoop, calls=%fused_computation.191 | loop fusion | flops 2064384 | bytes 1512000 | tf_op jit(solution)/shard_map/sub | solution.py:127
  39.3 0.6 collective-permute-start.13
  39.9 0.8 copy.315
  41.3 6.4 %collective-permute-done.9 = f32[10,1,16,128]{3,2,0,1:T(8,128)S(1)} collective-permute-done((f32[10,1,16,128]{3,2,0,1:T(8,128)S(1)}, f32[10,1,16,128]{3,2,0,1:T(8,128)S(1)}, u32[]{:S(2)}, u32[]{:S(2)}) %collective-permute-start.9) | collective-permute-done | bytes 81952 | tf_op jit(solution)/shard_map/ppermute | solution.py:64
  47.6 2.7 %collective-permute-start.10 = (f32[10,16,128]{2,1,0:T(8,128)S(1)}, f32[10,16,128]{2,1,0:T(8,128)S(1)}, u32[]{:S(2)}, u32[]{:S(2)}) collective-permute-start(f32[10,16,128]{2,1,0:T(8,128)S(1)} %bitcast.729), channel_id=1, source_target_pairs={{0,2},{2,4},{4,6},{6,0},{1,3},{3,5},{5,7},{7,1},{8,10},{10,12},{12... | collective-permute-start | bytes 245768 | tf_op jit(solution)/shard_map/ppermute | solution.py:45
  50.5 13.0 %all-gather.1 = f32[10,1,64,128]{3,1,0,2:T(1,128)S(1)} all-gather(f32[10,1,16,128]{3,1,0,2:T(1,128)S(1)} %copy.202), channel_id=3, replica_groups=mesh['gx'=32,'gy'=4,'gz'=2] {'gy'}, dimensions={2}, use_global_device_ids=true | all-gather | bytes 409600 | tf_op jit(solution)/shard_map/all_gather | solution.py:141
  63.5 0.1 maximum_bitcast_fusion.1
  63.7 2.9 %collective-permute-start.12 = (f32[10,16,128]{2,1,0:T(8,128)S(1)}, f32[10,16,128]{2,1,0:T(8,128)S(1)}, u32[]{:S(2)}, u32[]{:S(2)}) collective-permute-start(f32[10,16,128]{2,1,0:T(8,128)S(1)} %collective-permute-done.10), channel_id=1, source_target_pairs={{0,2},{2,4},{4,6},{6,0},{1,3},{3,5},{5,7},{7,1},{8,10},{10,12},{12... | collective-permute-start | bytes 245768 | tf_op jit(solution)/shard_map/ppermute | solution.py:45
  66.6 2.0 %collective-permute-done.12 = f32[10,16,128]{2,1,0:T(8,128)S(1)} collective-permute-done((f32[10,16,128]{2,1,0:T(8,128)S(1)}, f32[10,16,128]{2,1,0:T(8,128)S(1)}, u32[]{:S(2)}, u32[]{:S(2)}) %collective-permute-start.12) | collective-permute-done | bytes 81952 | tf_op jit(solution)/shard_map/ppermute | solution.py:45
  68.7 0.1 maximum_bitcast_fusion.2
  68.8 0.2 fusion
  69.0 3.7 %collective-permute-start.14 = (f32[38,6,1,128]{3,0,2,1:T(8,128)S(1)}, f32[38,6,1,128]{3,0,2,1:T(8,128)S(1)}, u32[]{:S(2)}, u32[]{:S(2)}) collective-permute-start(f32[38,6,1,128]{3,0,2,1:T(8,128)S(1)} %copy.222), channel_id=1, source_target_pairs={{0,2},{2,4},{4,6},{6,0},{1,3},{3,5},{5,7},{7,1},{8,10},{10,12},{12... | collective-permute-start | bytes 350216 | tf_op jit(solution)/shard_map/ppermute | solution.py:64
  72.8 2.3 %collective-permute-done.14 = f32[38,6,1,128]{3,0,2,1:T(8,128)S(1)} collective-permute-done((f32[38,6,1,128]{3,0,2,1:T(8,128)S(1)}, f32[38,6,1,128]{3,0,2,1:T(8,128)S(1)}, u32[]{:S(2)}, u32[]{:S(2)}) %collective-permute-start.14) | collective-permute-done | bytes 116768 | tf_op jit(solution)/shard_map/ppermute | solution.py:64
  75.2 0.1 copy.223
  75.3 3.6 %collective-permute-done.15 = f32[38,6,1,128]{3,0,2,1:T(8,128)S(1)} collective-permute-done((f32[38,6,1,128]{3,0,2,1:T(8,128)S(1)}, f32[38,6,1,128]{3,0,2,1:T(8,128)S(1)}, u32[]{:S(2)}, u32[]{:S(2)}) %collective-permute-start.15) | collective-permute-done | bytes 116768 | tf_op jit(solution)/shard_map/ppermute | solution.py:66
  78.9 0.1 copy.225
  79.0 0.4 pad_maximum_fusion
  79.5 3.2 %fusion.105 = (f32[38,6,18,1]{3,2,0,1:T(8,128)}, f32[38,6,18,1]{3,2,0,1:T(8,128)}) fusion(f32[38,6,18,128]{3,2,0,1:T(8,128)S(1)} %pad_maximum_fusion), kind=kLoop, calls=%fused_computation.408 | loop fusion | bytes 65664 | tf_op jit(solution)/shard_map/slice | solution.py:60
  82.7 2.9 %copy.228 = f32[38,6,18,1]{0,2,3,1:T(8,128)S(1)} copy(f32[38,6,18,1]{3,2,0,1:T(8,128)} %get-tuple-element.53) | data formatting | bytes 32832 | tf_op jit(solution)/shard_map/slice | solution.py:61
  85.6 4.6 %collective-permute-start.16 = (f32[38,6,18,1]{0,2,3,1:T(8,128)S(1)}, f32[38,6,18,1]{0,2,3,1:T(8,128)S(1)}, u32[]{:S(2)}, u32[]{:S(2)}) collective-permute-start(f32[38,6,18,1]{0,2,3,1:T(8,128)S(1)} %copy.228), channel_id=1, source_target_pairs={{0,1},{1,0},{2,3},{3,2},{4,5},{5,4},{6,7},{7,6},{8,9},{9,8},{10,11... | collective-permute-start | bytes 49256 | tf_op jit(solution)/shard_map/ppermute | solution.py:64
  90.2 2.9 %copy.230 = f32[38,6,18,1]{0,2,3,1:T(8,128)S(1)} copy(f32[38,6,18,1]{3,2,0,1:T(8,128)} %get-tuple-element.52) | data formatting | bytes 32832 | tf_op jit(solution)/shard_map/slice | solution.py:60
  93.1 1.5 %collective-permute-start.17 = (f32[38,6,18,1]{0,2,3,1:T(8,128)S(1)}, f32[38,6,18,1]{0,2,3,1:T(8,128)S(1)}, u32[]{:S(2)}, u32[]{:S(2)}) collective-permute-start(f32[38,6,18,1]{0,2,3,1:T(8,128)S(1)} %copy.230), channel_id=1, source_target_pairs={{1,0},{0,1},{3,2},{2,3},{5,4},{4,5},{7,6},{6,7},{9,8},{8,9},{11,10... | collective-permute-start | bytes 49256 | tf_op jit(solution)/shard_map/ppermute | solution.py:66
  94.6 0.1 collective-permute-done.16
  94.7 2.7 %copy.229 = f32[38,6,18,1]{3,2,0,1:T(8,128)} copy(f32[38,6,18,1]{0,2,3,1:T(8,128)S(1)} %collective-permute-done.16) | data formatting | bytes 32832 | tf_op jit(solution)/shard_map/ppermute | solution.py:64
  97.4 0.9 constant_dynamic-update-slice_fusion.91
  98.3 3.1 %collective-permute-done.17 = f32[38,6,18,1]{0,2,3,1:T(8,128)S(1)} collective-permute-done((f32[38,6,18,1]{0,2,3,1:T(8,128)S(1)}, f32[38,6,18,1]{0,2,3,1:T(8,128)S(1)}, u32[]{:S(2)}, u32[]{:S(2)}) %collective-permute-start.17) | collective-permute-done | bytes 16448 | tf_op jit(solution)/shard_map/ppermute | solution.py:66
  101.4 2.7 %copy.231 = f32[38,6,18,1]{3,2,0,1:T(8,128)} copy(f32[38,6,18,1]{0,2,3,1:T(8,128)S(1)} %collective-permute-done.17) | data formatting | bytes 32832 | tf_op jit(solution)/shard_map/ppermute | solution.py:66
  104.1 0.9 constant_dynamic-update-slice_fusion.90
  105.1 1.7 %copy-done.1 = f32[38,6,18,1]{3,2,0,1:T(8,128)S(1)} copy-done((f32[38,6,18,1]{3,2,0,1:T(8,128)S(1)}, f32[38,6,18,1]{3,2,0,1:T(8,128)}, u32[]{:S(2)}) %copy-start.1) | copy-done | bytes 16440
  106.9 1.7 %copy-done = f32[38,6,18,1]{3,2,0,1:T(8,128)S(1)} copy-done((f32[38,6,18,1]{3,2,0,1:T(8,128)S(1)}, f32[38,6,18,1]{3,2,0,1:T(8,128)}, u32[]{:S(2)}) %copy-start) | copy-done | bytes 16440
  108.9 1.0 copy-done.4
  109.9 0.1 constant_dynamic-update-slice_fusion.79
  110.3 0.1 constant_dynamic-update-slice_fusion.78
  110.7 0.9 copy.235
  111.8 0.1 constant_dynamic-update-slice_fusion.60
  112.1 0.9 copy.234
  (133 shorter events, 3.1 us)
Async XLA Ops:
  0.6 37.9 %copy-start.3 = (f32[19,4,16,128]{3,2,1,0:T(8,128)S(1)}, f32[19,4,16,128]{3,2,1,0:T(8,128)}, u32[]{:S(2)}) copy-start(f32[19,4,16,128]{3,2,1,0:T(8,128)} %param.4) | copy-start | bytes 1867780
  0.6 37.9 %copy-start.2 = (f32[19,4,16,128]{3,2,1,0:T(8,128)S(1)}, f32[19,4,16,128]{3,2,1,0:T(8,128)}, u32[]{:S(2)}) copy-start(f32[19,4,16,128]{3,2,1,0:T(8,128)} %param.3) | copy-start | bytes 1867780
  1.9 11.4 %collective-permute-start.6 = (f32[4,1,128]{2,1,0:T(1,128)S(1)}, f32[4,1,128]{2,1,0:T(1,128)S(1)}, u32[]{:S(2)}, u32[]{:S(2)}) collective-permute-start(f32[4,1,128]{2,1,0:T(1,128)S(1)} %get-tuple-element.98), channel_id=1, source_target_pairs={{2,0},{4,2},{6,4},{0,6},{3,1},{5,3},{7,5},{1,7},{10,8},{12,10},{14... | collective-permute-start | bytes 6152 | tf_op jit(solution)/shard_map/ppermute | solution.py:66
  2.8 10.5 %collective-permute-start.5 = (f32[4,1,128]{2,1,0:T(1,128)S(1)}, f32[4,1,128]{2,1,0:T(1,128)S(1)}, u32[]{:S(2)}, u32[]{:S(2)}) collective-permute-start(f32[4,1,128]{2,1,0:T(1,128)S(1)} %get-tuple-element.99), channel_id=1, source_target_pairs={{0,2},{2,4},{4,6},{6,0},{1,3},{3,5},{5,7},{7,1},{8,10},{10,12},{12... | collective-permute-start | bytes 6152 | tf_op jit(solution)/shard_map/ppermute | solution.py:64
  5.2 16.2 %collective-permute-start.4 = (f32[1,1,16,128]{3,2,1,0:T(8,128)S(1)}, f32[1,1,16,128]{3,2,1,0:T(8,128)S(1)}, u32[]{:S(2)}, u32[]{:S(2)}) collective-permute-start(f32[1,1,16,128]{3,2,1,0:T(8,128)S(1)} %get-tuple-element.104), channel_id=1, source_target_pairs={{8,0},{16,8},{24,16},{32,24},{40,32},{48,40},{56,48},{64,56},{72,6... | collective-permute-start | bytes 24584 | tf_op jit(solution)/shard_map/ppermute | solution.py:66
  11.2 8.2 %collective-permute-start = (f32[1,1,16,128]{3,2,1,0:T(8,128)S(1)}, f32[1,1,16,128]{3,2,1,0:T(8,128)S(1)}, u32[]{:S(2)}, u32[]{:S(2)}) collective-permute-start(f32[1,1,16,128]{3,2,1,0:T(8,128)S(1)} %get-tuple-element.105), channel_id=1, source_target_pairs={{0,8},{8,16},{16,24},{24,32},{32,40},{40,48},{48,56},{56,64},{64,7... | collective-permute-start | bytes 24584 | tf_op jit(solution)/shard_map/ppermute | solution.py:64
  13.4 23.7 %collective-permute-start.8 = (f32[4,18,1]{2,1,0:T(8,128)S(1)}, f32[4,18,1]{2,1,0:T(8,128)S(1)}, u32[]{:S(2)}, u32[]{:S(2)}) collective-permute-start(f32[4,18,1]{2,1,0:T(8,128)S(1)} %get-tuple-element.96), channel_id=1, source_target_pairs={{1,0},{0,1},{3,2},{2,3},{5,4},{4,5},{7,6},{6,7},{9,8},{8,9},{11,10... | collective-permute-start | bytes 872 | tf_op jit(solution)/shard_map/ppermute | solution.py:66
  17.9 19.2 %collective-permute-start.7 = (f32[4,18,1]{2,1,0:T(8,128)S(1)}, f32[4,18,1]{2,1,0:T(8,128)S(1)}, u32[]{:S(2)}, u32[]{:S(2)}) collective-permute-start(f32[4,18,1]{2,1,0:T(8,128)S(1)} %get-tuple-element.97), channel_id=1, source_target_pairs={{0,1},{1,0},{2,3},{3,2},{4,5},{5,4},{6,7},{7,6},{8,9},{9,8},{10,11... | collective-permute-start | bytes 872 | tf_op jit(solution)/shard_map/ppermute | solution.py:64
  19.4 14.0 %collective-permute-start.1 = (f32[1,16,128]{2,1,0:T(8,128)S(1)}, f32[1,16,128]{2,1,0:T(8,128)S(1)}, u32[]{:S(2)}, u32[]{:S(2)}) collective-permute-start(f32[1,16,128]{2,1,0:T(8,128)S(1)} %bitcast.731), channel_id=1, source_target_pairs={{0,2},{2,4},{4,6},{6,0},{1,3},{3,5},{5,7},{7,1},{8,10},{10,12},{12... | collective-permute-start | bytes 24584 | tf_op jit(solution)/shard_map/ppermute | solution.py:45
  19.7 15.3 %collective-permute-start.2 = (f32[1,16,128]{2,1,0:T(8,128)S(1)}, f32[1,16,128]{2,1,0:T(8,128)S(1)}, u32[]{:S(2)}, u32[]{:S(2)}) collective-permute-start(f32[1,16,128]{2,1,0:T(8,128)S(1)} %bitcast.732), channel_id=1, source_target_pairs={{0,6},{2,0},{4,2},{6,4},{1,7},{3,1},{5,3},{7,5},{8,14},{10,8},{12,... | collective-permute-start | bytes 24584 | tf_op jit(solution)/shard_map/ppermute | solution.py:48
  33.4 3.7 %collective-permute-start.3 = (f32[1,16,128]{2,1,0:T(8,128)S(1)}, f32[1,16,128]{2,1,0:T(8,128)S(1)}, u32[]{:S(2)}, u32[]{:S(2)}) collective-permute-start(f32[1,16,128]{2,1,0:T(8,128)S(1)} %collective-permute-done.1), channel_id=1, source_target_pairs={{0,2},{2,4},{4,6},{6,0},{1,3},{3,5},{5,7},{7,1},{8,10},{10,12},{12... | collective-permute-start | bytes 24584 | tf_op jit(solution)/shard_map/ppermute | solution.py:45
  39.3 11.1 %collective-permute-start.13 = (f32[10,1,16,128]{3,2,0,1:T(8,128)S(1)}, f32[10,1,16,128]{3,2,0,1:T(8,128)S(1)}, u32[]{:S(2)}, u32[]{:S(2)}) collective-permute-start(f32[10,1,16,128]{3,2,0,1:T(8,128)S(1)} %get-tuple-element.82), channel_id=1, source_target_pairs={{8,0},{16,8},{24,16},{32,24},{40,32},{48,40},{56,48},{64,56},{72,6... | collective-permute-start | bytes 245768 | tf_op jit(solution)/shard_map/ppermute | solution.py:66
  39.9 7.8 %collective-permute-start.9 = (f32[10,1,16,128]{3,2,0,1:T(8,128)S(1)}, f32[10,1,16,128]{3,2,0,1:T(8,128)S(1)}, u32[]{:S(2)}, u32[]{:S(2)}) collective-permute-start(f32[10,1,16,128]{3,2,0,1:T(8,128)S(1)} %get-tuple-element.83), channel_id=1, source_target_pairs={{0,8},{8,16},{16,24},{24,32},{32,40},{40,48},{48,56},{56,64},{64,7... | collective-permute-start | bytes 245768 | tf_op jit(solution)/shard_map/ppermute | solution.py:64
  47.6 16.0 %collective-permute-start.10 = (f32[10,16,128]{2,1,0:T(8,128)S(1)}, f32[10,16,128]{2,1,0:T(8,128)S(1)}, u32[]{:S(2)}, u32[]{:S(2)}) collective-permute-start(f32[10,16,128]{2,1,0:T(8,128)S(1)} %bitcast.729), channel_id=1, source_target_pairs={{0,2},{2,4},{4,6},{6,0},{1,3},{3,5},{5,7},{7,1},{8,10},{10,12},{12... | collective-permute-start | bytes 245768 | tf_op jit(solution)/shard_map/ppermute | solution.py:45
  50.4 16.3 %collective-permute-start.11 = (f32[10,16,128]{2,1,0:T(8,128)S(1)}, f32[10,16,128]{2,1,0:T(8,128)S(1)}, u32[]{:S(2)}, u32[]{:S(2)}) collective-permute-start(f32[10,16,128]{2,1,0:T(8,128)S(1)} %bitcast.730), channel_id=1, source_target_pairs={{0,6},{2,0},{4,2},{6,4},{1,7},{3,1},{5,3},{7,5},{8,14},{10,8},{12,... | collective-permute-start | bytes 245768 | tf_op jit(solution)/shard_map/ppermute | solution.py:48
  63.7 5.0 %collective-permute-start.12 = (f32[10,16,128]{2,1,0:T(8,128)S(1)}, f32[10,16,128]{2,1,0:T(8,128)S(1)}, u32[]{:S(2)}, u32[]{:S(2)}) collective-permute-start(f32[10,16,128]{2,1,0:T(8,128)S(1)} %collective-permute-done.10), channel_id=1, source_target_pairs={{0,2},{2,4},{4,6},{6,0},{1,3},{3,5},{5,7},{7,1},{8,10},{10,12},{12... | collective-permute-start | bytes 245768 | tf_op jit(solution)/shard_map/ppermute | solution.py:45
  69.0 6.1 %collective-permute-start.14 = (f32[38,6,1,128]{3,0,2,1:T(8,128)S(1)}, f32[38,6,1,128]{3,0,2,1:T(8,128)S(1)}, u32[]{:S(2)}, u32[]{:S(2)}) collective-permute-start(f32[38,6,1,128]{3,0,2,1:T(8,128)S(1)} %copy.222), channel_id=1, source_target_pairs={{0,2},{2,4},{4,6},{6,0},{1,3},{3,5},{5,7},{7,1},{8,10},{10,12},{12... | collective-permute-start | bytes 350216 | tf_op jit(solution)/shard_map/ppermute | solution.py:64
  72.7 6.2 %collective-permute-start.15 = (f32[38,6,1,128]{3,0,2,1:T(8,128)S(1)}, f32[38,6,1,128]{3,0,2,1:T(8,128)S(1)}, u32[]{:S(2)}, u32[]{:S(2)}) collective-permute-start(f32[38,6,1,128]{3,0,2,1:T(8,128)S(1)} %copy.224), channel_id=1, source_target_pairs={{2,0},{4,2},{6,4},{0,6},{3,1},{5,3},{7,5},{1,7},{10,8},{12,10},{14... | collective-permute-start | bytes 350216 | tf_op jit(solution)/shard_map/ppermute | solution.py:66
  85.6 9.1 %collective-permute-start.16 = (f32[38,6,18,1]{0,2,3,1:T(8,128)S(1)}, f32[38,6,18,1]{0,2,3,1:T(8,128)S(1)}, u32[]{:S(2)}, u32[]{:S(2)}) collective-permute-start(f32[38,6,18,1]{0,2,3,1:T(8,128)S(1)} %copy.228), channel_id=1, source_target_pairs={{0,1},{1,0},{2,3},{3,2},{4,5},{5,4},{6,7},{7,6},{8,9},{9,8},{10,11... | collective-permute-start | bytes 49256 | tf_op jit(solution)/shard_map/ppermute | solution.py:64
  93.1 8.3 %collective-permute-start.17 = (f32[38,6,18,1]{0,2,3,1:T(8,128)S(1)}, f32[38,6,18,1]{0,2,3,1:T(8,128)S(1)}, u32[]{:S(2)}, u32[]{:S(2)}) collective-permute-start(f32[38,6,18,1]{0,2,3,1:T(8,128)S(1)} %copy.230), channel_id=1, source_target_pairs={{1,0},{0,1},{3,2},{2,3},{5,4},{4,5},{7,6},{6,7},{9,8},{8,9},{11,10... | collective-permute-start | bytes 49256 | tf_op jit(solution)/shard_map/ppermute | solution.py:66
  105.0 1.8 %copy-start.1 = (f32[38,6,18,1]{3,2,0,1:T(8,128)S(1)}, f32[38,6,18,1]{3,2,0,1:T(8,128)}, u32[]{:S(2)}) copy-start(f32[38,6,18,1]{3,2,0,1:T(8,128)} %copy.231) | copy-start | bytes 49252
  106.8 1.8 %copy-start = (f32[38,6,18,1]{3,2,0,1:T(8,128)S(1)}, f32[38,6,18,1]{3,2,0,1:T(8,128)}, u32[]{:S(2)}) copy-start(f32[38,6,18,1]{3,2,0,1:T(8,128)} %copy.229) | copy-start | bytes 49252
  108.8 1.1 copy-start.4
